TPU v7x, 32 devices: a whole 2x2x4 slice. The times are simulated.
32 devices in a mesh: req: 8 (over z, x), grp: 4 (over y, core).
Axes of the slice: x: 2, y: 2, z: 4, core: 2. Of those that a mesh axis runs over, the one named last changes fastest.
Arguments:
- residual: bfloat16 [8192, 2048], P('req', 'grp'), may hold values from -6 to 6
- queries: bfloat16 [8192, 2048], P('req', 'grp'), may hold values from -26 to 26
- new_keys: bfloat16 [8192, 512], P('req', 'grp'), may hold values from -26 to 26
- new_values: bfloat16 [8192, 512], P('req', 'grp'), may hold values from -6 to 6
- pool_keys: bfloat16 [36864, 512], P('req', 'grp'), may hold values from -6 to 6
- pool_values: bfloat16 [36864, 512], P('req', 'grp'), may hold values from -6 to 6
- cache_len: int32 [64], P('req'), may hold values from 1 to 512, as said below
- prefix_group: int32 [64], P('req'), may hold values from 0 to 7, as said below
- prefix_len: int32 [64], P('req'), may hold values from 0 to 512, as said below
- span_rows: int32 [8], replicated, may hold values from 0 to 1008, as said below
- span_offset: int32 [8], P('req'), may hold values from 0 to 512
- out_weight: bfloat16 [2048, 2048], P('grp'), may hold values from -0.125 to 0.125
- norm_gain: float32 [2048], replicated, may hold values from 0.1 to 1.9
- gate_weight: bfloat16 [2048, 4096], P(None, 'grp'), may hold values from -0.125 to 0.125
- up_weight: bfloat16 [2048, 4096], P(None, 'grp'), may hold values from -0.125 to 0.125
- down_weight: bfloat16 [4096, 2048], P('grp'), may hold values from -0.09375 to 0.09375
Outputs:
- layer_out: bfloat16 [8192, 2048], P('req', 'grp')
Inputs may be any that keep to these rules, and one draw needn't show every extreme that they name: `cache_len`: the first decode request of every req index has a cache of 512 positions. `prefix_group`: the slot, within its req index, of the first request of the group; at or before the request's own slot; a group's requests stand in consecutive slots. `prefix_len`: equal within a group and at most the cache length of each of its requests; some request shares 512 positions. `span_rows`: exactly 4 req indices hold a span of 1008 rows, the others none.
All inputs are finite; a program needn't handle non-finite values.
Results may differ from a plain program's by a relative error of at most 0.014.
Values may be sent and summed in bfloat16 or wider, within the bound.
No kernel may reach another device: no remote copies, remote signals or barrier semaphores. Data moves between devices by JAX's collectives and lax.ppermute only.
A program may use at most 128 MiB of HBM per device.

v0:
```python
import jax
import jax.numpy as jnp
from jax import lax
from jax.sharding import PartitionSpec as P

HEADS = 32
KV_HEADS = 8
HEAD_DIM = 64
DEC = 8
BAL = 512
REG = 512
MASKED_SCORE = -1e30


def attend(query_rows, key_rows, value_rows, allowed):
    scores = jnp.dot(query_rows, key_rows.T, preferred_element_type=jnp.float32) * query_rows.shape[
        1
    ] ** (-0.5)
    scores = jnp.where(allowed, scores, MASKED_SCORE)
    highest = jnp.max(scores, axis=1, keepdims=True)
    expval = jnp.exp(scores - highest)
    totals = jnp.sum(expval, axis=1, keepdims=True)
    probs = (expval / totals).astype(jnp.bfloat16)
    return jnp.dot(probs, value_rows, preferred_element_type=jnp.float32).astype(jnp.bfloat16)


def build_masks(cache_len, prefix_group, prefix_len, span_count, span_start, total_rows):
    position = jnp.arange(DEC * REG, dtype=jnp.int32)
    region = position // REG
    offset = position % REG
    request = jnp.arange(DEC, dtype=jnp.int32)
    shared = (region[None, :] == prefix_group[:, None]) & (offset[None, :] < prefix_len[:, None])
    owned = (
        (region[None, :] == request[:, None])
        & (offset[None, :] >= prefix_len[:, None])
        & (offset[None, :] < cache_len[:, None])
    )
    decode_mask = jnp.concatenate([shared | owned, jnp.eye(DEC, dtype=jnp.bool_)], axis=1)
    span_total = total_rows - DEC
    within = jnp.arange(span_total, dtype=jnp.int32)
    in_span = within < span_count
    earlier = jnp.arange(REG, dtype=jnp.int32)
    prior = (earlier[None, :] < span_start) & in_span[:, None]
    lowest = jnp.where(in_span, 0, within)
    causal = (within[None, :] >= lowest[:, None]) & (within[None, :] <= within[:, None])
    span_mask = jnp.concatenate([prior, causal], axis=1)
    return (decode_mask, span_mask)


def attention(queries, new_keys, new_values, pool_keys, pool_values, decode_mask, span_mask):
    head_count = queries.shape[1] // HEAD_DIM
    per_kv = HEADS // KV_HEADS
    split_at = DEC * REG

    def one_head(head):
        query_rows = lax.dynamic_slice_in_dim(queries, head * HEAD_DIM, HEAD_DIM, 1)
        column = head // per_kv * HEAD_DIM
        fresh_keys = lax.dynamic_slice_in_dim(new_keys, column, HEAD_DIM, 1)
        fresh_values = lax.dynamic_slice_in_dim(new_values, column, HEAD_DIM, 1)
        cached_keys = lax.dynamic_slice_in_dim(pool_keys, column, HEAD_DIM, 1)
        cached_values = lax.dynamic_slice_in_dim(pool_values, column, HEAD_DIM, 1)
        decode_out = attend(
            query_rows[:DEC],
            jnp.concatenate([cached_keys[:split_at], fresh_keys[:DEC]], axis=0),
            jnp.concatenate([cached_values[:split_at], fresh_values[:DEC]], axis=0),
            decode_mask,
        )
        span_out = attend(
            query_rows[DEC:],
            jnp.concatenate([cached_keys[split_at:], fresh_keys[DEC:]], axis=0),
            jnp.concatenate([cached_values[split_at:], fresh_values[DEC:]], axis=0),
            span_mask,
        )
        return jnp.concatenate([decode_out, span_out], axis=0)

    outputs = lax.map(one_head, jnp.arange(head_count, dtype=jnp.int32))
    return jnp.transpose(outputs, (1, 0, 2)).reshape(queries.shape[0], head_count * HEAD_DIM)


def finish(attn_rows, resid_rows, out_weight, norm_gain, gate_weight, up_weight, down_weight):
    partial_value = jnp.dot(attn_rows, out_weight, preferred_element_type=jnp.float32)
    proj_cols = lax.psum_scatter(
        partial_value.astype(jnp.bfloat16), "grp", scatter_dimension=1, tiled=True
    ).astype(jnp.float32)
    state_cols = (resid_rows.astype(jnp.float32) + proj_cols).astype(jnp.bfloat16)
    state_full = lax.all_gather(state_cols, "grp", axis=1, tiled=True)
    state32 = state_full.astype(jnp.float32)
    normed = (
        state32 * lax.rsqrt(jnp.mean(state32 * state32, axis=1, keepdims=True) + 1e-05) * norm_gain
    ).astype(jnp.bfloat16)
    gate = jnp.dot(normed, gate_weight, preferred_element_type=jnp.float32)
    upval = jnp.dot(normed, up_weight, preferred_element_type=jnp.float32)
    inner = (jax.nn.silu(gate) * upval).astype(jnp.bfloat16)
    down_cols = lax.psum_scatter(
        jnp.dot(inner, down_weight, preferred_element_type=jnp.float32).astype(jnp.bfloat16),
        "grp",
        scatter_dimension=1,
        tiled=True,
    ).astype(jnp.float32)
    return (state_cols.astype(jnp.float32) + down_cols).astype(jnp.bfloat16)


def shards(
    residual,
    queries,
    new_keys,
    new_values,
    pool_keys,
    pool_values,
    cache_len,
    prefix_group,
    prefix_len,
    span_rows,
    span_offset,
    out_weight,
    norm_gain,
    gate_weight,
    up_weight,
    down_weight,
):
    total_rows = residual.shape[0]
    width = residual.shape[1]
    device = lax.axis_index("req")
    devices = lax.axis_size("req")
    own_span = span_rows[device]
    decode_mask, span_mask = build_masks(
        cache_len, prefix_group, prefix_len, own_span, span_offset[0], total_rows
    )
    attn = attention(queries, new_keys, new_values, pool_keys, pool_values, decode_mask, span_mask)
    row_index = jnp.arange(total_rows, dtype=jnp.int32)
    is_live = row_index < DEC + own_span
    zero_value = jnp.zeros((), jnp.bfloat16)
    counts = DEC + span_rows
    first = jnp.sum(jnp.where(jnp.arange(devices, dtype=jnp.int32) < device, counts, 0))
    target = jnp.where(is_live, first + row_index, -1)
    bucket = (total_rows - DEC + devices - 1) // devices
    owner_dev = jnp.where(is_live, target % devices, devices)
    bucket_pos = jnp.where(is_live, row_index // devices, 0)
    send_attn = (
        jnp.zeros((devices, bucket, width), jnp.bfloat16)
        .at[owner_dev, bucket_pos]
        .set(attn, mode="drop")
    )
    send_resid = (
        jnp.zeros((devices, bucket, width), jnp.bfloat16)
        .at[owner_dev, bucket_pos]
        .set(residual, mode="drop")
    )
    send_target = (
        jnp.full((devices, bucket), -1, jnp.int32)
        .at[owner_dev, bucket_pos]
        .set(target, mode="drop")
    )
    got_attn, got_resid, got_target = (
        lax.all_to_all(send_attn, "req", split_axis=0, concat_axis=0, tiled=True),
        lax.all_to_all(send_resid, "req", split_axis=0, concat_axis=0, tiled=True),
        lax.all_to_all(send_target, "req", split_axis=0, concat_axis=0, tiled=True),
    )
    flat_target = got_target.reshape(-1)
    has_row = flat_target >= 0
    bal_slot = jnp.where(has_row, flat_target // devices, BAL)
    dense_attn = (
        jnp.zeros((BAL, width), jnp.bfloat16)
        .at[bal_slot]
        .set(got_attn.reshape(-1, width), mode="drop")
    )
    dense_resid = (
        jnp.zeros((BAL, width), jnp.bfloat16)
        .at[bal_slot]
        .set(got_resid.reshape(-1, width), mode="drop")
    )
    mixed = finish(
        dense_attn, dense_resid, out_weight, norm_gain, gate_weight, up_weight, down_weight
    )
    picked = jnp.where(has_row[:, None], mixed[jnp.minimum(bal_slot, BAL - 1)], zero_value)
    returned = lax.all_to_all(
        picked.reshape(devices, bucket, width), "req", split_axis=0, concat_axis=0, tiled=True
    )
    layer_out = jnp.where(
        is_live[:, None], returned[jnp.minimum(owner_dev, devices - 1), bucket_pos], zero_value
    )
    return layer_out


def solution(mesh):
    placed = (
        P("req", "grp"),
        P("req", "grp"),
        P("req", "grp"),
        P("req", "grp"),
        P("req", "grp"),
        P("req", "grp"),
        P("req"),
        P("req"),
        P("req"),
        P(),
        P("req"),
        P("grp", None),
        P(),
        P(None, "grp"),
        P(None, "grp"),
        P("grp", None),
    )
    return jax.shard_map(
        shards, mesh=mesh, in_specs=placed, out_specs=P("req", "grp"), check_vma=False
    )
```

profile of v0, /device:TPU:0, one launch (start us, length us, event | category | flops | bytes accessed | tf_op | source)
XLA Modules:
  0.0 414.9 jit_solution(9925079914877743265)
XLA Ops:
  13.4 4.3 %scatter_custom_fusion.2 = s32[1016]{0:T(1024)S(1)} fusion(s32[1024]{0:T(1024)S(1)} %get-tuple-element.165, s32[1024]{0:T(1024)S(1)} %add_select_fusion.1, s32[]{:T(128)} %constant.165.clone.1), kind=kCustom, calls=%fused_computation.122 | custom fusion | bytes 4068
  18.4 7.3 %all-to-all-start = ((s32[8,1,127]{2,1,0:T(1,128)}), s32[8,1,127]{2,1,0:T(1,128)}, u32[]{:S(2)}, u32[]{:S(2)}) async-start(s32[8,1,127]{2,1,0:T(1,128)} %bitcast.3), calls=%async_computation | async-start | bytes 8192 | tf_op jit(solution)/shard_map/all_to_all | solution.py:157
  32.1 151.4 %while.12 = (s32[]{:T(128)}, bf16[8,1024,64]{1,2,0:T(8,128)(2,1)}, s32[8]{0:T(128)}, bf16[1024,512]{1,0:T(8,128)(2,1)}, bf16[4608,128]{1,0:T(8,128)(2,1)S(1)}, /...) while((s32[]{:T(128)}, bf16[8,1024,64]{1,2,0:T(8,128)(2,1)}, ...), condition=%wide.region_9.10_spmd, body=%wide.region_4.9_spmd.sunk | while | flops 421723168 | bytes 31715728 | solution.py:76
  38.5 3.2 fusion.80
  43.2 2.2 fusion.82
  57.4 3.2 fusion.80
  76.4 3.2 fusion.80
  95.3 3.2 fusion.80
  114.2 3.2 fusion.80
  133.2 3.2 fusion.80
  137.9 2.2 fusion.82
  152.1 3.2 fusion.80
  171.0 3.2 fusion.80
  183.5 2.3 copy.35
  185.8 5.8 %scatter_custom_fusion.4 = bf16[1016,512]{1,0:T(8,128)(2,1)S(1)} fusion(s32[1024]{0:T(1024)} %get-tuple-element.164, bf16[1024,512]{1,0:T(8,128)(2,1)} %copy.35, bf16[]{:T(256)} %constant.170.clone.1), kind=kCustom, calls=%fused_computation.64 | custom fusion | bytes 1040896
  192.9 6.0 %all-to-all-start.2 = ((bf16[8,127,512]{2,1,0:T(8,128)(2,1)}), bf16[8,127,512]{2,1,0:T(8,128)(2,1)S(1)}, u32[]{:S(2)}, u32[]{:S(2)}) async-start(bf16[8,127,512]{2,1,0:T(8,128)(2,1)} %copy.36), calls=%async_computation.2 | async-start | bytes 2097152 | tf_op jit(solution)/shard_map/all_to_all | solution.py:155
  201.1 23.3 %all-to-all-done.2 = bf16[8,127,512]{2,1,0:T(8,128)(2,1)S(1)} async-done(((bf16[8,127,512]{2,1,0:T(8,128)(2,1)}), bf16[8,127,512]{2,1,0:T(8,128)(2,1)S(1)}, u32[]{:S(2)}, u32[]{:S(2)}) %all-to-all-start.2) | async-done | bytes 1040416 | tf_op jit(solution)/shard_map/all_to_all | solution.py:155
  225.6 6.3 %scatter_custom_fusion.1 = bf16[512,512]{1,0:T(8,128)(2,1)S(1)} fusion(s32[1016]{0:T(1024)S(1)} %bitcast.38, bf16[1016,512]{1,0:T(8,128)(2,1)} %reshape.365, bf16[]{:T(256)} %constant.170.clone.1), kind=kCustom, calls=%fused_computation.68 | custom fusion | bytes 524800 | tf_op jit(solution)/shard_map/scatter | solution.py:165
  232.0 2.6 convolution_convert_fusion.2
  234.7 5.8 %scatter_custom_fusion.3 = bf16[1016,512]{1,0:T(8,128)(2,1)S(1)} fusion(s32[1024]{0:T(1024)} %get-tuple-element.164, bf16[1024,512]{1,0:T(8,128)(2,1)} %param.18, bf16[]{:T(256)} %constant.170.clone.1), kind=kCustom, calls=%fused_computation.66 | custom fusion | bytes 1040896
  240.9 29.1 %all_to_all.24 = bf16[8,127,512]{2,1,0:T(8,128)(2,1)S(1)} all-to-all(bf16[8,127,512]{2,1,0:T(8,128)(2,1)S(1)} %copy.34), channel_id=1, replica_groups=mesh['req'=8,'grp'=4] {'req'}, dimensions={0} | all-to-all | bytes 2080768 | tf_op jit(solution)/shard_map/all_to_all | solution.py:156
  271.2 6.3 %scatter_custom_fusion = bf16[512,512]{1,0:T(8,128)(2,1)S(1)} fusion(s32[1016]{0:T(1024)S(1)} %bitcast.39, bf16[1016,512]{1,0:T(8,128)(2,1)} %reshape.357, bf16[]{:T(256)} %constant.170.clone.1), kind=kCustom, calls=%fused_computation.70 | custom fusion | bytes 524800 | tf_op jit(solution)/shard_map/scatter | solution.py:170
  279.9 21.6 %all-gather.2.cloned.1.call-done = bf16[512,2048]{1,0:T(8,128)(2,1)} async-done(((bf16[512,512]{1,0:T(8,128)(2,1)}), bf16[512,2048]{1,0:T(8,128)(2,1)}) %all-gather.2.cloned.1.call-update) | async-done | bytes 2097168 | tf_op jit(solution)/shard_map/all_gather | solution.py:86
  301.4 2.2 fusion.27
  303.7 5.9 %fusion.33 = f32[512,1024]{1,0:T(8,128)} fusion(bf16[2048,1024]{1,0:T(8,128)(2,1)} %param.31, bf16[512,2048]{1,0:T(8,128)(2,1)S(1)} %copy-done.6, f32[2048]{0:T(1024)S(1)} %copy-done.8, f32[512]{0:T(512)S(1)} %add_rsqrt_fusion), kind=kOutput, calls=%fused_computation.63 | convolution fusion | flops 2151677952 | bytes 8398848 | tf_op jit(solution)/shard_map/dot_general | solution.py:91
  309.6 10.6 %convolution_convert_fusion.1 = bf16[512,2048]{1,0:T(8,128)(2,1)} fusion(bf16[1024,2048]{1,0:T(8,128)(2,1)} %param.33, f32[512,1024]{1,0:T(8,128)} %fusion.33, bf16[2048,1024]{1,0:T(8,128)(2,1)} %param.32, bf16[512,2048]{1,0:T(8,128)(2,1)} %all-gather.2.cloned.1.call-done, f32[2048]{0:T(1024)S(1)} %copy-done.8, f32[512]{0:T(512)S(1)} %add_rsqrt_fusion), kind=kOutput, calls=%fused_computation.55 | convolution fusion | flops 4303355904 | bytes 14690304 | tf_op jit(solution)/shard_map/dot_general | solution.py:95
  321.0 30.8 %reduce-scatter.5.cloned.1.call-done = bf16[512,512]{1,0:T(8,128)(2,1)} async-done(((bf16[512,2048]{1,0:T(8,128)(2,1)}), bf16[512,512]{1,0:T(8,128)(2,1)}) %reduce-scatter.5.cloned.1.call-update) | async-done | bytes 524304 | tf_op jit(solution)/shard_map/reduce_scatter | solution.py:94
  353.0 5.1 %gather_fusion = bf16[1016,512]{1,0:T(8,128)(2,1)} fusion(bf16[512,512]{1,0:T(8,128)(2,1)S(1)} %add_convert_fusion, s32[1024]{0:T(1024)S(1)} %pad_clamp_fusion), kind=kCustom, calls=%fused_computation | custom fusion | bytes 2084832 | tf_op jit(solution)/shard_map/gather | solution.py:175
  360.8 5.5 %all-to-all-start.3 = ((bf16[8,127,512]{2,1,0:T(8,128)(2,1)}), bf16[8,127,512]{2,1,0:T(8,128)(2,1)}, u32[]{:S(2)}, u32[]{:S(2)}) async-start(bf16[8,127,512]{2,1,0:T(8,128)(2,1)} %broadcast_select_fusion.1), calls=%async_computation.5 | async-start | bytes 2097152 | tf_op jit(solution)/shard_map/all_to_all | solution.py:176
  367.0 25.2 %all-to-all-done.3 = bf16[8,127,512]{2,1,0:T(8,128)(2,1)} async-done(((bf16[8,127,512]{2,1,0:T(8,128)(2,1)}), bf16[8,127,512]{2,1,0:T(8,128)(2,1)}, u32[]{:S(2)}, u32[]{:S(2)}) %all-to-all-start.3) | async-done | bytes 1040416 | tf_op jit(solution)/shard_map/all_to_all | solution.py:176
  394.0 12.0 %gather_fusion.1 = bf16[1024,512]{1,0:T(8,128)(2,1)} fusion(bf16[8,127,512]{2,0,1:T(8,128)(2,1)S(1)} %copy.37, s32[1024]{0:T(1024)S(1)} %bitcast.33), kind=kCustom, calls=%fused_computation.1 | custom fusion | bytes 2105344 | tf_op jit(solution)/shard_map/gather | solution.py:180
  406.0 2.4 broadcast_select_fusion
  (217 shorter events, 121.3 us)
Async XLA Ops:
  6.5 225.5 %copy-start = (bf16[512,2048]{1,0:T(8,128)(2,1)S(1)}, bf16[512,2048]{1,0:T(8,128)(2,1)}, u32[]{:S(2)}) copy-start(bf16[512,2048]{1,0:T(8,128)(2,1)} %param.29) | copy-start | bytes 6291460
  18.4 174.6 %all-to-all-start = ((s32[8,1,127]{2,1,0:T(1,128)}), s32[8,1,127]{2,1,0:T(1,128)}, u32[]{:S(2)}, u32[]{:S(2)}) async-start(s32[8,1,127]{2,1,0:T(1,128)} %bitcast.3), calls=%async_computation | async-start | bytes 8192 | tf_op jit(solution)/shard_map/all_to_all | solution.py:157
  27.6 4.5 %copy-start.1 = (bf16[4608,128]{1,0:T(8,128)(2,1)S(1)}, bf16[4608,128]{1,0:T(8,128)(2,1)}, u32[]{:S(2)}) copy-start(bf16[4608,128]{1,0:T(8,128)(2,1)} %param.22) | copy-start | bytes 3538948
  27.6 4.5 %copy-start.3 = (bf16[1024,128]{1,0:T(8,128)(2,1)S(1)}, bf16[1024,128]{1,0:T(8,128)(2,1)}, u32[]{:S(2)}) copy-start(bf16[1024,128]{1,0:T(8,128)(2,1)} %param.20) | copy-start | bytes 786436
  41.8 1.0 copy-start.4
  41.8 1.4 copy-start.2
  45.5 0.8 copy-start.7
  60.7 1.0 copy-start.4
  60.7 1.4 copy-start.2
  64.4 0.8 copy-start.7
  79.6 1.0 copy-start.4
  79.6 1.4 copy-start.2
  83.3 0.8 copy-start.7
  98.5 1.0 copy-start.4
  98.5 1.4 copy-start.2
  117.5 1.0 copy-start.4
  117.5 1.4 copy-start.2
  136.4 1.0 copy-start.4
  136.4 1.4 copy-start.2
  140.1 0.8 copy-start.7
  155.3 1.0 copy-start.4
  155.3 1.4 copy-start.2
  174.2 1.0 copy-start.4
  174.3 1.4 copy-start.2
  192.9 31.4 %all-to-all-start.2 = ((bf16[8,127,512]{2,1,0:T(8,128)(2,1)}), bf16[8,127,512]{2,1,0:T(8,128)(2,1)S(1)}, u32[]{:S(2)}, u32[]{:S(2)}) async-start(bf16[8,127,512]{2,1,0:T(8,128)(2,1)} %copy.36), calls=%async_computation.2 | async-start | bytes 2097152 | tf_op jit(solution)/shard_map/all_to_all | solution.py:155
  198.9 78.7 %reduce-scatter.3.cloned.1.call-start = ((), (), s32[]{:S(2)}) async-start(), calls=%async_computation.6 | async-start | bytes 2621440 | tf_op jit(solution)/shard_map/reduce_scatter | solution.py:82
  234.7 66.8 %all-gather.2.cloned.1.call-start = ((), (), s32[]{:S(2)}) async-start(), calls=%async_computation.7 | async-start | bytes 2621440 | tf_op jit(solution)/shard_map/all_gather | solution.py:86
  277.6 26.1 %copy-start.8 = (f32[2048]{0:T(1024)S(1)}, f32[2048]{0:T(1024)}, u32[]{:S(2)}) copy-start(f32[2048]{0:T(1024)} %param.30) | copy-start | bytes 24580
  279.6 72.3 %reduce-scatter.5.cloned.1.call-start = ((), (), s32[]{:S(2)}) async-start(), calls=%async_computation.8 | async-start | bytes 2621440 | tf_op jit(solution)/shard_map/reduce_scatter | solution.py:94
  301.4 2.2 copy-start.6
  320.2 31.6 %copy-start.5 = (bf16[512,512]{1,0:T(8,128)(2,1)S(1)}, bf16[512,512]{1,0:T(8,128)(2,1)}, u32[]{:S(2)}) copy-start(bf16[512,512]{1,0:T(8,128)(2,1)} %add_convert_fusion.1) | copy-start | bytes 1572868
  360.8 31.4 %all-to-all-start.3 = ((bf16[8,127,512]{2,1,0:T(8,128)(2,1)}), bf16[8,127,512]{2,1,0:T(8,128)(2,1)}, u32[]{:S(2)}, u32[]{:S(2)}) async-start(bf16[8,127,512]{2,1,0:T(8,128)(2,1)} %broadcast_select_fusion.1), calls=%async_computation.5 | async-start | bytes 2097152 | tf_op jit(solution)/shard_map/all_to_all | solution.py:176
  (4 other events, 3.0 us)
Sparse Core Ops, SparseCore 0:
  234.8 30.2 reduce-scatter.2
  279.7 21.6 all-gather.1
  320.4 31.4 reduce-scatter.4
where the time goes:
time: 418 us; the launch traced here: 415 us
  waiting for transfers between devices  101 us (24%)
  local copies, waits for them, and re-layouts  98.6 us (24%)
  matrix products  79.5 us (19%)
  other arithmetic  44.7 us (11%)
  blocking collectives  29.1 us (7%)
  loops' own time  28.2 us (7%)
  starting transfers between devices  19.1 us (5%)
  between operations  14.8 us (4%)
    dot_general x16, matrix products, attend(): jnp.dot(query_rows, key_rows.T, preferred_element_type=jnp.float32)  35.5 us
    reduce_scatter x1, waiting for transfers between devices, finish(): lax.psum_scatter(jnp.dot(inner, down_weight, preferred_element_type=jnp.f...  30.8 us
    all_to_all x1, blocking collectives, shards(): lax.all_to_all(send_resid, 'req', split_axis=0, concat_axis=0, tiled=True)  29.1 us
    another operation x1, loops' own time, attention(): outputs = lax.map(one_head, jnp.arange(head_count, dtype=jnp.int32))  28.2 us
    all_to_all x1, waiting for transfers between devices, shards(): lax.all_to_all(picked.reshape(devices, bucket, width), 'req', split_axis=...  25.2 us
    dot_general x16, matrix products, attend(): jnp.dot(probs, value_rows, preferred_element_type=jnp.float32)  24.8 us
    all_to_all x1, waiting for transfers between devices, shards(): lax.all_to_all(send_attn, 'req', split_axis=0, concat_axis=0, tiled=True)  23.3 us
    all_gather x1, waiting for transfers between devices, finish(): state_full = lax.all_gather(state_cols, 'grp', axis=1, tiled=True)  21.6 us
  transfers between devices with their start and end apart: 6, of which 4 were waited for; matrix products, arithmetic and copies ran while one was open for 37% of the time, Pallas kernels for 0%

commit v1 on v0

--- a/solution.py
+++ b/solution.py
@@ -2,6 +2,7 @@
 import jax.numpy as jnp
 from jax import lax
 from jax.sharding import PartitionSpec as P
+from jax.lax import axis_index, axis_size, ppermute
 
 HEADS = 32
 KV_HEADS = 8
@@ -83,7 +84,18 @@
         partial_value.astype(jnp.bfloat16), "grp", scatter_dimension=1, tiled=True
     ).astype(jnp.float32)
     state_cols = (resid_rows.astype(jnp.float32) + proj_cols).astype(jnp.bfloat16)
-    state_full = lax.all_gather(state_cols, "grp", axis=1, tiled=True)
+    step_out = axis_size("grp")
+    x_now = axis_index("grp")
+    carry_in, odd = (step_out, x_now)
+    state_full, e_now = (state_cols, 1)
+    while e_now < carry_in:
+        mat_out = ppermute(
+            state_full, axis_name="grp", perm=[(nth, nth ^ e_now) for nth in range(carry_in)]
+        )
+        vec_out = jnp.concatenate([state_full, mat_out], 1)
+        piece_next = jnp.concatenate([mat_out, state_full], 1)
+        state_full = jnp.where(odd & e_now == 0, vec_out, piece_next)
+        e_now = 2 * e_now
     state32 = state_full.astype(jnp.float32)
     normed = (
         state32 * lax.rsqrt(jnp.mean(state32 * state32, axis=1, keepdims=True) + 1e-05) * norm_gain

time: 418 us -> 426 us (1.019)
    ppermute x0 -> x2, waiting for transfers between devices: none -> 25.9 us  [finish(): ppermute(state_full, axis_name='grp', perm=[(nth, nth ^ e_now) for nth in...]
    all_gather x1 -> x0, waiting for transfers between devices: 21.6 us -> none  [finish(): state_full = lax.all_gather(state_cols, 'grp', axis=1, tiled=True)]
    unnamed x15 -> x11, local copies, waits for them, and re-layouts: 16 us -> 16 us
  transfers between devices with their start and end apart: 6 -> 7, of which waited for: 4 -> 5; matrix products, arithmetic and copies ran while one was open for 37% -> 36% of each run, Pallas kernels for 0% -> 0%
where the time goes in v1:
time: 426 us; the launch traced here: 423 us
  waiting for transfers between devices  104 us (24%)
  local copies, waits for them, and re-layouts  98.8 us (23%)
  matrix products  81.4 us (19%)
  other arithmetic  45.9 us (11%)
  blocking collectives  29.1 us (7%)
  loops' own time  28.2 us (7%)
  starting transfers between devices  20.4 us (5%)
  between operations  15.1 us (4%)
    dot_general x16, matrix products, attend(): jnp.dot(query_rows, key_rows.T, preferred_element_type=jnp.float32)  35.5 us
    reduce_scatter x1, waiting for transfers between devices, finish(): lax.psum_scatter(jnp.dot(inner, down_weight, preferred_element_type=jnp.f...  30 us
    all_to_all x1, blocking collectives, shards(): lax.all_to_all(send_resid, 'req', split_axis=0, concat_axis=0, tiled=True)  29.1 us
    another operation x1, loops' own time, attention(): outputs = lax.map(one_head, jnp.arange(head_count, dtype=jnp.int32))  28.2 us
    ppermute x2, waiting for transfers between devices, finish(): ppermute(state_full, axis_name='grp', perm=[(nth, nth ^ e_now) for nth in...  25.9 us
    all_to_all x1, waiting for transfers between devices, shards(): lax.all_to_all(picked.reshape(devices, bucket, width), 'req', split_axis=...  25.2 us
    dot_general x16, matrix products, attend(): jnp.dot(probs, value_rows, preferred_element_type=jnp.float32)  24.8 us
    all_to_all x1, waiting for transfers between devices, shards(): lax.all_to_all(send_attn, 'req', split_axis=0, concat_axis=0, tiled=True)  23.3 us
  transfers between devices with their start and end apart: 7, of which 5 were waited for; matrix products, arithmetic and copies ran while one was open for 36% of the time, Pallas kernels for 0%

profile of v1, /device:TPU:0, one launch (start us, length us, event | category | flops | bytes accessed | tf_op | source)
XLA Modules:
  0.0 423.4 jit_solution(845612251730111521)
XLA Ops:
  13.4 4.3 %scatter_custom_fusion.2 = s32[1016]{0:T(1024)S(1)} fusion(s32[1024]{0:T(1024)S(1)} %get-tuple-element.165, s32[1024]{0:T(1024)S(1)} %add_select_fusion.1, s32[]{:T(128)} %constant.169.clone.1), kind=kCustom, calls=%fused_computation.124 | custom fusion | bytes 4068
  18.4 7.3 %all-to-all-start = ((s32[8,1,127]{2,1,0:T(1,128)}), s32[8,1,127]{2,1,0:T(1,128)}, u32[]{:S(2)}, u32[]{:S(2)}) async-start(s32[8,1,127]{2,1,0:T(1,128)} %bitcast.3), calls=%async_computation | async-start | bytes 8192 | tf_op jit(solution)/shard_map/all_to_all | solution.py:169
  32.2 151.4 %while.12 = (s32[]{:T(128)}, bf16[8,1024,64]{1,2,0:T(8,128)(2,1)}, s32[8]{0:T(128)}, bf16[1024,512]{1,0:T(8,128)(2,1)}, bf16[4608,128]{1,0:T(8,128)(2,1)S(1)}, /...) while((s32[]{:T(128)}, bf16[8,1024,64]{1,2,0:T(8,128)(2,1)}, ...), condition=%wide.region_9.10_spmd, body=%wide.region_4.9_spmd.sunk | while | flops 421723168 | bytes 31715728 | solution.py:77
  38.6 3.2 fusion.80
  43.3 2.2 fusion.82
  57.5 3.2 fusion.80
  76.4 3.2 fusion.80
  95.3 3.2 fusion.80
  100.1 2.2 fusion.82
  114.3 3.2 fusion.80
  133.2 3.2 fusion.80
  152.1 3.2 fusion.80
  171.0 3.2 fusion.80
  183.6 2.3 copy.35
  185.9 5.8 %scatter_custom_fusion.4 = bf16[1016,512]{1,0:T(8,128)(2,1)S(1)} fusion(s32[1024]{0:T(1024)} %get-tuple-element.164, bf16[1024,512]{1,0:T(8,128)(2,1)} %copy.35, bf16[]{:T(256)} %constant.174.clone.1), kind=kCustom, calls=%fused_computation.66 | custom fusion | bytes 1040896
  193.0 6.0 %all-to-all-start.2 = ((bf16[8,127,512]{2,1,0:T(8,128)(2,1)}), bf16[8,127,512]{2,1,0:T(8,128)(2,1)S(1)}, u32[]{:S(2)}, u32[]{:S(2)}) async-start(bf16[8,127,512]{2,1,0:T(8,128)(2,1)} %copy.36), calls=%async_computation.2 | async-start | bytes 2097152 | tf_op jit(solution)/shard_map/all_to_all | solution.py:167
  201.1 23.3 %all-to-all-done.2 = bf16[8,127,512]{2,1,0:T(8,128)(2,1)S(1)} async-done(((bf16[8,127,512]{2,1,0:T(8,128)(2,1)}), bf16[8,127,512]{2,1,0:T(8,128)(2,1)S(1)}, u32[]{:S(2)}, u32[]{:S(2)}) %all-to-all-start.2) | async-done | bytes 1040416 | tf_op jit(solution)/shard_map/all_to_all | solution.py:167
  225.7 6.3 %scatter_custom_fusion.1 = bf16[512,512]{1,0:T(8,128)(2,1)S(1)} fusion(s32[1016]{0:T(1024)S(1)} %bitcast.38, bf16[1016,512]{1,0:T(8,128)(2,1)} %reshape.365, bf16[]{:T(256)} %constant.174.clone.1), kind=kCustom, calls=%fused_computation.70 | custom fusion | bytes 524800 | tf_op jit(solution)/shard_map/scatter | solution.py:177
  232.1 2.6 convolution_convert_fusion.2
  234.7 5.8 %scatter_custom_fusion.3 = bf16[1016,512]{1,0:T(8,128)(2,1)S(1)} fusion(s32[1024]{0:T(1024)} %get-tuple-element.164, bf16[1024,512]{1,0:T(8,128)(2,1)} %param.18, bf16[]{:T(256)} %constant.174.clone.1), kind=kCustom, calls=%fused_computation.68 | custom fusion | bytes 1040896
  240.9 29.1 %all_to_all.24 = bf16[8,127,512]{2,1,0:T(8,128)(2,1)S(1)} all-to-all(bf16[8,127,512]{2,1,0:T(8,128)(2,1)S(1)} %copy.34), channel_id=1, replica_groups=mesh['req'=8,'grp'=4] {'req'}, dimensions={0} | all-to-all | bytes 2080768 | tf_op jit(solution)/shard_map/all_to_all | solution.py:168
  271.2 6.6 %scatter_custom_fusion = bf16[512,512]{1,0:T(8,128)(2,1)S(1)} fusion(s32[1016]{0:T(1024)S(1)} %bitcast.39, bf16[1016,512]{1,0:T(8,128)(2,1)} %reshape.357, bf16[]{:T(256)} %constant.174.clone.1), kind=kCustom, calls=%fused_computation.72 | custom fusion | bytes 524800 | tf_op jit(solution)/shard_map/scatter | solution.py:182
  283.8 24.0 %collective-permute-done.1 = bf16[512,1024]{1,0:T(8,128)(2,1)} collective-permute-done((bf16[512,1024]{1,0:T(8,128)(2,1)}, bf16[512,1024]{1,0:T(8,128)(2,1)}, u32[]{:S(2)}, u32[]{:S(2)}) %collective-permute-start.1) | collective-permute-done | bytes 1048608 | tf_op jit(solution)/shard_map/ppermute | solution.py:92
  307.8 3.0 fusion.27
  310.8 7.2 %fusion.33 = f32[512,1024]{1,0:T(8,128)} fusion(bf16[2048,1024]{1,0:T(8,128)(2,1)} %param.31, f32[2048]{0:T(1024)S(1)} %copy-done.6, f32[512]{0:T(512)S(1)} %add_rsqrt_fusion, bf16[512,1024]{1,0:T(8,128)(2,1)} %collective-permute-done.1, bf16[512,1024]{1,0:T(8,128)(2,1)} %maximum_select_fusion.1, pred[]{:T(512)S(6)} %eq.45), kind=kOutput, calls=%fused_computation.65 | convolution fusion | flops 2161115136 | bytes 8398849 | tf_op jit(solution)/shard_map/dot_general | solution.py:103
  318.0 11.3 %convolution_convert_fusion.1 = bf16[512,2048]{1,0:T(8,128)(2,1)} fusion(bf16[1024,2048]{1,0:T(8,128)(2,1)} %param.33, f32[512,1024]{1,0:T(8,128)} %fusion.33, bf16[2048,1024]{1,0:T(8,128)(2,1)} %param.32, f32[2048]{0:T(1024)S(1)} %copy-done.6, f32[512]{0:T(512)S(1)} %add_rsqrt_fusion, bf16[512,1024]{1,0:T(8,128)(2,1)} %collective-permute-done.1, ...), kind=kOutput, calls=%fused_computation.55 | convolution fusion | flops 4312793088 | bytes 14690305 | tf_op jit(solution)/shard_map/dot_general | solution.py:107
  330.0 30.0 %reduce-scatter.5.cloned.1.call-done = bf16[512,512]{1,0:T(8,128)(2,1)} async-done(((bf16[512,2048]{1,0:T(8,128)(2,1)}), bf16[512,512]{1,0:T(8,128)(2,1)}) %reduce-scatter.5.cloned.1.call-update) | async-done | bytes 524304 | tf_op jit(solution)/shard_map/reduce_scatter | solution.py:106
  361.2 5.1 %gather_fusion = bf16[1016,512]{1,0:T(8,128)(2,1)} fusion(bf16[512,512]{1,0:T(8,128)(2,1)S(1)} %add_convert_fusion, s32[1024]{0:T(1024)S(1)} %pad_clamp_fusion), kind=kCustom, calls=%fused_computation | custom fusion | bytes 2084832 | tf_op jit(solution)/shard_map/gather | solution.py:187
  369.0 5.5 %all-to-all-start.3 = ((bf16[8,127,512]{2,1,0:T(8,128)(2,1)}), bf16[8,127,512]{2,1,0:T(8,128)(2,1)}, u32[]{:S(2)}, u32[]{:S(2)}) async-start(bf16[8,127,512]{2,1,0:T(8,128)(2,1)} %broadcast_select_fusion.1), calls=%async_computation.5 | async-start | bytes 2097152 | tf_op jit(solution)/shard_map/all_to_all | solution.py:188
  375.2 25.2 %all-to-all-done.3 = bf16[8,127,512]{2,1,0:T(8,128)(2,1)} async-done(((bf16[8,127,512]{2,1,0:T(8,128)(2,1)}), bf16[8,127,512]{2,1,0:T(8,128)(2,1)}, u32[]{:S(2)}, u32[]{:S(2)}) %all-to-all-start.3) | async-done | bytes 1040416 | tf_op jit(solution)/shard_map/all_to_all | solution.py:188
  402.2 12.0 %gather_fusion.1 = bf16[1024,512]{1,0:T(8,128)(2,1)} fusion(bf16[8,127,512]{2,0,1:T(8,128)(2,1)S(1)} %copy.37, s32[1024]{0:T(1024)S(1)} %bitcast.33), kind=kCustom, calls=%fused_computation.1 | custom fusion | bytes 2105344 | tf_op jit(solution)/shard_map/gather | solution.py:192
  414.1 2.4 broadcast_select_fusion
  (215 shorter events, 124.8 us)
Async XLA Ops:
  6.5 225.5 %copy-start = (bf16[512,2048]{1,0:T(8,128)(2,1)S(1)}, bf16[512,2048]{1,0:T(8,128)(2,1)}, u32[]{:S(2)}) copy-start(bf16[512,2048]{1,0:T(8,128)(2,1)} %param.29) | copy-start | bytes 6291460
  18.4 174.6 %all-to-all-start = ((s32[8,1,127]{2,1,0:T(1,128)}), s32[8,1,127]{2,1,0:T(1,128)}, u32[]{:S(2)}, u32[]{:S(2)}) async-start(s32[8,1,127]{2,1,0:T(1,128)} %bitcast.3), calls=%async_computation | async-start | bytes 8192 | tf_op jit(solution)/shard_map/all_to_all | solution.py:169
  27.6 4.5 %copy-start.1 = (bf16[4608,128]{1,0:T(8,128)(2,1)S(1)}, bf16[4608,128]{1,0:T(8,128)(2,1)}, u32[]{:S(2)}) copy-start(bf16[4608,128]{1,0:T(8,128)(2,1)} %param.22) | copy-start | bytes 3538948
  27.7 4.5 %copy-start.3 = (bf16[1024,128]{1,0:T(8,128)(2,1)S(1)}, bf16[1024,128]{1,0:T(8,128)(2,1)}, u32[]{:S(2)}) copy-start(bf16[1024,128]{1,0:T(8,128)(2,1)} %param.20) | copy-start | bytes 786436
  41.8 1.0 copy-start.4
  41.8 1.4 copy-start.2
  45.5 0.8 copy-start.5
  60.7 1.0 copy-start.4
  60.7 1.4 copy-start.2
  64.4 0.8 copy-start.5
  79.6 1.0 copy-start.4
  79.7 1.4 copy-start.2
  83.4 0.8 copy-start.5
  98.6 1.0 copy-start.4
  98.6 1.4 copy-start.2
  102.3 0.8 copy-start.5
  117.5 1.0 copy-start.4
  117.5 1.4 copy-start.2
  121.2 0.8 copy-start.5
  136.4 1.0 copy-start.4
  136.4 1.4 copy-start.2
  155.4 1.0 copy-start.4
  155.4 1.4 copy-start.2
  174.3 1.0 copy-start.4
  174.3 1.4 copy-start.2
  193.0 31.4 %all-to-all-start.2 = ((bf16[8,127,512]{2,1,0:T(8,128)(2,1)}), bf16[8,127,512]{2,1,0:T(8,128)(2,1)S(1)}, u32[]{:S(2)}, u32[]{:S(2)}) async-start(bf16[8,127,512]{2,1,0:T(8,128)(2,1)} %copy.36), calls=%async_computation.2 | async-start | bytes 2097152 | tf_op jit(solution)/shard_map/all_to_all | solution.py:167
  199.0 78.9 %reduce-scatter.3.cloned.1.call-start = ((), (), s32[]{:S(2)}) async-start(), calls=%async_computation.6 | async-start | bytes 2621440 | tf_op jit(solution)/shard_map/reduce_scatter | solution.py:83
  234.7 125.3 %reduce-scatter.5.cloned.1.call-start = ((), (), s32[]{:S(2)}) async-start(), calls=%async_computation.7 | async-start | bytes 2621440 | tf_op jit(solution)/shard_map/reduce_scatter | solution.py:106
  279.0 2.0 collective-permute-start
  279.1 31.7 %copy-start.6 = (f32[2048]{0:T(1024)S(1)}, f32[2048]{0:T(1024)}, u32[]{:S(2)}) copy-start(f32[2048]{0:T(1024)} %param.30) | copy-start | bytes 24580
  282.3 25.5 %collective-permute-start.1 = (bf16[512,1024]{1,0:T(8,128)(2,1)}, bf16[512,1024]{1,0:T(8,128)(2,1)}, u32[]{:S(2)}, u32[]{:S(2)}) collective-permute-start(bf16[512,1024]{1,0:T(8,128)(2,1)} %maximum_select_fusion.1), channel_id=1, source_target_pairs={{0,2},{1,3},{2,0},{3,1},{4,6},{5,7},{6,4},{7,5},{8,10},{9,11},{10,... | collective-permute-start | bytes 3145736 | tf_op jit(solution)/shard_map/ppermute | solution.py:92
  369.0 31.4 %all-to-all-start.3 = ((bf16[8,127,512]{2,1,0:T(8,128)(2,1)}), bf16[8,127,512]{2,1,0:T(8,128)(2,1)}, u32[]{:S(2)}, u32[]{:S(2)}) async-start(bf16[8,127,512]{2,1,0:T(8,128)(2,1)} %broadcast_select_fusion.1), calls=%async_computation.5 | async-start | bytes 2097152 | tf_op jit(solution)/shard_map/all_to_all | solution.py:188
  (3 other events, 2.3 us)
Sparse Core Ops, SparseCore 0:
  234.8 30.2 reduce-scatter.2
  329.4 30.4 reduce-scatter.4
